TPU v7x, 32 devices: a whole 2x2x4 slice. The times are simulated.
32 devices in a mesh: outer: 4 (over y, core), inner: 8 (over z, x).
Axes of the slice: x: 2, y: 2, z: 4, core: 2. Of those that a mesh axis runs over, the one named last changes fastest.
Arguments:
- token_ids: int32 [32768], P(('outer', 'inner')), may hold values from 0 to 50303, as said below
- inner_x: bfloat16 [32768, 512], P(('outer', 'inner')), may hold values from -6 to 6
- out_gate: bfloat16 [32768, 512], P(('outer', 'inner')), may hold values from -6 to 6
- gate_pre: float32 [2, 32768], P(None, ('outer', 'inner')), may hold values from -4 to 300
- conv_weight: float32 [4, 512], replicated, may hold values from -3 to 3
- qkv_weight: bfloat16 [3, 4, 4, 128], replicated, may hold values from -3 to 3
- norm_gain: float32 [512], replicated, may hold values from 0.1 to 1.9
- skip_gain: float32 [512], replicated, may hold values from 0.1 to 1.9
Outputs:
- gated_out: bfloat16 [32768, 512], P(('outer', 'inner'))
Inputs may be any that keep to these rules, and one draw needn't show every extreme that they name: `token_ids`: A token with id 0 is a document delimiter: it starts a new document, and no earlier token reaches it or any later token.
All inputs are finite; a program needn't handle non-finite values.
Results may differ from a plain program's by a relative error of at most 0.012.
The roundings to bfloat16 on the way count: a program that leaves them out, or rounds other values in their place, can miss the bound.
Values may be sent and summed in bfloat16 or wider, within the bound.
No kernel may reach another device: no remote copies, remote signals or barrier semaphores. Data moves between devices by JAX's collectives and lax.ppermute only.
A program may use at most 64 MiB of HBM per device.

v0:
```python
import jax
import jax.numpy as jnp
from jax import lax
from jax.sharding import PartitionSpec as P

HIGHEST = lax.Precision.HIGHEST


def passed_along(shard, axis, by):
    size = lax.axis_size(axis)
    pairs = [(i, i + by) for i in range(size) if 0 <= i + by < size]
    return lax.ppermute(shard, axis, pairs)


def dense_blocks(block_table, channels):
    group_size = block_table.shape[0]
    index_rows = jnp.arange(channels)
    same_block = index_rows[:, None] // group_size == index_rows[None, :] // group_size
    lane_phase = index_rows % group_size
    dense_matrix = jnp.zeros((channels, channels), jnp.float32)
    for column in range(group_size):
        column_values = block_table[:, column, :].T.reshape(channels).astype(jnp.float32)
        dense_matrix = dense_matrix + column_values[:, None] * (lane_phase[None, :] == column)
    return jnp.where(same_block, dense_matrix, 0.0).astype(block_table.dtype)


def combine(earlier, later):
    memory_first, level_first, decay_first, cut_first = earlier
    memory_second, level_second, decay_second, cut_second = later
    kept_level = jnp.where(cut_second > 0.5, -jnp.inf, level_first + decay_second)
    new_level = jnp.maximum(kept_level, level_second)
    safe_level = jnp.where(new_level == -jnp.inf, 0.0, new_level)
    new_memory = (
        jnp.exp(kept_level - safe_level) * memory_first
        + jnp.exp(level_second - safe_level) * memory_second
    )
    return (new_memory, new_level, decay_first + decay_second, jnp.maximum(cut_first, cut_second))


def prefix_before(state, identity, count, token_position, mover):
    distances = [1]
    reach = 1
    while reach < count - 1:
        distances.append(reach)
        reach = reach * 2
    current = state
    for step_number, distance in enumerate(distances):
        arrived = mover(current, distance)
        present = token_position >= distance
        arrived = tuple(
            (jnp.where(present, piece, blank) for piece, blank in zip(arrived, identity))
        )
        if step_number == 0:
            current = arrived
        else:
            current = combine(arrived, current)
    return current


def body(token_ids, inner_x, out_gate, gate_pre, conv_weight, qkv_weight, norm_gain, skip_gain):
    num_rows, channels = inner_x.shape
    kernel_taps = conv_weight.shape[0]
    rim_rows = passed_along(inner_x[num_rows - kernel_taps + 1 :], ("outer", "inner"), 1)
    extended = jnp.concatenate([rim_rows, inner_x], axis=0)
    conv_sum = jnp.zeros((num_rows, channels), jnp.float32)
    for offset in range(kernel_taps):
        conv_sum = conv_sum + conv_weight[offset] * extended[offset : offset + num_rows].astype(
            jnp.float32
        )
    convolved = jax.nn.silu(conv_sum).astype(jnp.bfloat16)
    query_rows = jnp.dot(
        convolved, dense_blocks(qkv_weight[0], channels), preferred_element_type=jnp.float32
    ).astype(jnp.bfloat16)
    key_rows = (
        jnp.dot(
            convolved, dense_blocks(qkv_weight[1], channels), preferred_element_type=jnp.float32
        )
        * channels ** (-0.5)
    ).astype(jnp.bfloat16)
    value_rows = jnp.dot(
        inner_x, dense_blocks(qkv_weight[2], channels), preferred_element_type=jnp.float32
    ).astype(jnp.bfloat16)
    input_gate = gate_pre[0]
    log_decay = jnp.cumsum(jax.nn.log_sigmoid(gate_pre[1]))
    doc_marks = jnp.cumsum((token_ids == 0).astype(jnp.int32))
    last_mark = doc_marks[num_rows - 1]
    value_float = value_rows.astype(jnp.float32)
    tail_weight = jnp.where(
        doc_marks == last_mark, log_decay[num_rows - 1] - log_decay + input_gate, -jnp.inf
    )
    tail_level = jnp.max(tail_weight)
    weighted_keys = jnp.exp(tail_weight - tail_level)[:, None] * key_rows.astype(jnp.float32)
    summary = lax.dot_general(
        weighted_keys, value_float, (((0,), (0,)), ((), ())), precision=HIGHEST
    )
    own_state = (summary, tail_level, log_decay[num_rows - 1], (last_mark > 0).astype(jnp.float32))
    identity = (
        jnp.zeros_like(summary),
        jnp.array(-jnp.inf, jnp.float32),
        jnp.array(0.0, jnp.float32),
        jnp.array(0.0, jnp.float32),
    )
    incoming = prefix_before(
        own_state,
        identity,
        lax.axis_size(("outer", "inner")),
        lax.axis_index(("outer", "inner")),
        lambda state, distance: passed_along(state, ("outer", "inner"), distance),
    )
    token_position = jnp.arange(num_rows)
    valid = (token_position[None, :] <= token_position[:, None]) & (
        doc_marks[None, :] == doc_marks[:, None]
    )
    log_weight = jnp.where(
        valid, log_decay[:, None] - log_decay[None, :] + input_gate[None, :], -jnp.inf
    )
    local_max = jnp.max(log_weight, axis=1)
    scores = lax.dot_general(
        query_rows, key_rows, (((1,), (1,)), ((), ())), preferred_element_type=jnp.float32
    )
    weights = jnp.exp(log_weight - local_max[:, None]) * scores
    local_sum = jnp.dot(weights, value_float, precision=HIGHEST)
    carried = jnp.where(doc_marks == 0, log_decay + incoming[1], -jnp.inf)
    row_max = jnp.maximum(carried, local_max)
    from_memory = jnp.dot(query_rows.astype(jnp.float32), incoming[0], precision=HIGHEST)
    retrieved = (
        jnp.exp(carried - row_max)[:, None] * from_memory
        + jnp.exp(local_max - row_max)[:, None] * local_sum
    )
    average = jnp.mean(retrieved, axis=1, keepdims=True)
    centered = retrieved - average
    variance = jnp.mean(centered * centered, axis=1, keepdims=True)
    normed = centered * lax.rsqrt(variance + 1e-05) * norm_gain
    gated_rows = (normed + skip_gain * convolved.astype(jnp.float32)) * jax.nn.silu(
        out_gate.astype(jnp.float32)
    )
    return gated_rows.astype(jnp.bfloat16)


def solution(mesh):
    return jax.shard_map(
        body,
        mesh=mesh,
        in_specs=(
            P(("outer", "inner")),
            P(("outer", "inner"), None),
            P(("outer", "inner"), None),
            P(None, ("outer", "inner")),
            P(),
            P(),
            P(),
            P(),
        ),
        out_specs=P(("outer", "inner"), None),
        check_vma=False,
    )
```

profile of v0, /device:TPU:0, one launch (start us, length us, event | category | flops | bytes accessed | tf_op | source)
XLA Modules:
  0.0 274.8 jit_solution(528736047582366060)
XLA Ops:
  0.0 0.8 slice.105
  0.8 0.2 copy.31
  1.0 4.9 %collective-permute-start.16 = (bf16[3,512]{0,1:T(8,128)(2,1)S(1)}, bf16[3,512]{0,1:T(8,128)(2,1)S(1)}, u32[]{:S(2)}, u32[]{:S(2)}) collective-permute-start(bf16[3,512]{0,1:T(8,128)(2,1)S(1)} %copy.31), channel_id=1, source_target_pairs={{0,1},{1,2},{2,3},{3,4},{4,5},{5,6},{6,7},{7,8},{8,9},{9,10},{10,1... | collective-permute-start | bytes 9224 | tf_op jit(solution)/shard_map/ppermute | solution.py:12
  5.8 0.7 convert_bitcast_fusion
  6.5 0.3 reduce-window.16
  6.9 0.1 slice_reduce_fusion.1
  7.1 0.7 slice.101
  8.5 4.7 %collective-permute-start = (f32[]{:T(128)}, f32[]{:T(128)}, u32[]{:S(2)}, u32[]{:S(2)}) collective-permute-start(f32[]{:T(128)} %convert_element_type.300), channel_id=1, source_target_pairs={{0,1},{1,2},{2,3},{3,4},{4,5},{5,6},{6,7},{7,8},{8,9},{9,10},{10,1... | collective-permute-start | bytes 20 | tf_op jit(solution)/shard_map/ppermute | solution.py:12
  13.2 0.7 slice_negate_fusion
  13.9 0.3 reduce-window.24
  14.3 0.1 slice_reduce_fusion
  14.5 0.6 slice.102
  15.1 3.9 %collective-permute-start.7 = (f32[]{:T(128)}, f32[]{:T(128)}, u32[]{:S(2)}, u32[]{:S(2)}) collective-permute-start(f32[]{:T(128)} %bitcast.5), channel_id=1, source_target_pairs={{0,1},{1,2},{2,3},{3,4},{4,5},{5,6},{6,7},{7,8},{8,9},{9,10},{10,1... | collective-permute-start | bytes 20 | tf_op jit(solution)/shard_map/ppermute | solution.py:12
  19.0 0.7 add_subtract_fusion
  19.7 0.8 compare_bitcast_fusion
  20.5 1.3 fusion.79
  21.8 3.5 %collective-permute-start.5 = (f32[]{:T(128)}, f32[]{:T(128)}, u32[]{:S(2)}, u32[]{:S(2)}) collective-permute-start(f32[]{:T(128)} %get-tuple-element.11), channel_id=1, source_target_pairs={{0,1},{1,2},{2,3},{3,4},{4,5},{5,6},{6,7},{7,8},{8,9},{9,10},{10,1... | collective-permute-start | bytes 20 | tf_op jit(solution)/shard_map/ppermute | solution.py:12
  25.4 1.5 copy.32
  27.0 0.1 copy.45
  27.2 0.1 copy.44
  28.7 1.8 fusion.4
  30.6 2.2 convolution_convert_fusion
  33.5 4.1 %collective-permute-start.1 = (f32[]{:T(128)}, f32[]{:T(128)}, u32[]{:S(2)}, u32[]{:S(2)}) collective-permute-start(f32[]{:T(128)} %select_n.231), channel_id=1, source_target_pairs={{0,1},{1,2},{2,3},{3,4},{4,5},{5,6},{6,7},{7,8},{8,9},{9,10},{10,1... | collective-permute-start | bytes 20 | tf_op jit(solution)/shard_map/ppermute | solution.py:12
  38.2 4.7 %collective-permute-start.6 = (f32[]{:T(128)}, f32[]{:T(128)}, u32[]{:S(2)}, u32[]{:S(2)}) collective-permute-start(f32[]{:T(128)} %select_n.237), channel_id=1, source_target_pairs={{0,1},{1,2},{2,3},{3,4},{4,5},{5,6},{6,7},{7,8},{8,9},{9,10},{10,1... | collective-permute-start | bytes 20 | tf_op jit(solution)/shard_map/ppermute | solution.py:12
  43.6 4.7 %collective-permute-start.9 = (f32[]{:T(128)}, f32[]{:T(128)}, u32[]{:S(2)}, u32[]{:S(2)}) collective-permute-start(f32[]{:T(128)} %select_n.239), channel_id=1, source_target_pairs={{0,1},{1,2},{2,3},{3,4},{4,5},{5,6},{6,7},{7,8},{8,9},{9,10},{10,1... | collective-permute-start | bytes 20 | tf_op jit(solution)/shard_map/ppermute | solution.py:12
  48.9 2.6 collective-permute-start.2
  52.2 3.6 %collective-permute-start.8 = (f32[]{:T(128)}, f32[]{:T(128)}, u32[]{:S(2)}, u32[]{:S(2)}) collective-permute-start(f32[]{:T(128)} %max.54), channel_id=1, source_target_pairs={{0,2},{1,3},{2,4},{3,5},{4,6},{5,7},{6,8},{7,9},{8,10},{9,11},{10,... | collective-permute-start | bytes 20 | tf_op jit(solution)/shard_map/ppermute | solution.py:12
  56.3 3.6 %collective-permute-start.11 = (f32[]{:T(128)}, f32[]{:T(128)}, u32[]{:S(2)}, u32[]{:S(2)}) collective-permute-start(f32[]{:T(128)} %add.206), channel_id=1, source_target_pairs={{0,2},{1,3},{2,4},{3,5},{4,6},{5,7},{6,8},{7,9},{8,10},{9,11},{10,... | collective-permute-start | bytes 20 | tf_op jit(solution)/shard_map/ppermute | solution.py:12
  60.6 3.7 %collective-permute-start.3 = (f32[]{:T(128)}, f32[]{:T(128)}, u32[]{:S(2)}, u32[]{:S(2)}) collective-permute-start(f32[]{:T(128)} %max.51), channel_id=1, source_target_pairs={{0,4},{1,5},{2,6},{3,7},{4,8},{5,9},{6,10},{7,11},{8,12},{9,13},{1... | collective-permute-start | bytes 20 | tf_op jit(solution)/shard_map/ppermute | solution.py:12
  64.9 5.4 %collective-permute-start.10 = (f32[]{:T(128)}, f32[]{:T(128)}, u32[]{:S(2)}, u32[]{:S(2)}) collective-permute-start(f32[]{:T(128)} %max.55), channel_id=1, source_target_pairs={{0,4},{1,5},{2,6},{3,7},{4,8},{5,9},{6,10},{7,11},{8,12},{9,13},{1... | collective-permute-start | bytes 20 | tf_op jit(solution)/shard_map/ppermute | solution.py:12
  71.0 5.9 %collective-permute-start.13 = (f32[]{:T(128)}, f32[]{:T(128)}, u32[]{:S(2)}, u32[]{:S(2)}) collective-permute-start(f32[]{:T(128)} %add.208), channel_id=1, source_target_pairs={{0,4},{1,5},{2,6},{3,7},{4,8},{5,9},{6,10},{7,11},{8,12},{9,13},{1... | collective-permute-start | bytes 20 | tf_op jit(solution)/shard_map/ppermute | solution.py:12
  77.6 2.2 collective-permute-start.4
  80.4 2.2 collective-permute-start.12
  83.3 2.1 collective-permute-start.15
  86.7 2.6 collective-permute-start.14
  90.6 2.0 fusion.72
  92.6 2.1 multiply_convert_fusion.1
  94.7 1.0 multiply_convert_fusion
  95.7 0.5 copy-done.10
  96.3 3.7 %fusion.12 = f32[512,512]{1,0:T(8,128)S(1)} fusion(bf16[512,1024]{1,0:T(8,128)(2,1)S(1)} %copy-done.10, bf16[1024,512]{1,0:T(8,128)(2,1)S(1)} %multiply_convert_fusion, f32[1024]{0:T(1024)S(1)} %get-tuple-element.10), kind=kOutput, calls=%fused_computation.17 | convolution fusion | flops 3222274048 | bytes 3149824 | tf_op jit(solution)/shard_map/dot_general | solution.py:93
  99.9 2.0 collective-permute-start.17
  102.0 21.1 %collective-permute-done.17 = f32[512,512]{1,0:T(8,128)S(1)} collective-permute-done((f32[512,512]{1,0:T(8,128)S(1)}, f32[512,512]{1,0:T(8,128)S(1)}, u32[]{:S(2)}, u32[]{:S(2)}) %collective-permute-start.17) | collective-permute-done | bytes 1048608 | tf_op jit(solution)/shard_map/ppermute | solution.py:12
  123.2 4.5 %collective-permute-start.18 = (f32[512,512]{1,0:T(8,128)S(1)}, f32[512,512]{1,0:T(8,128)S(1)}, u32[]{:S(2)}, u32[]{:S(2)}) collective-permute-start(f32[512,512]{1,0:T(8,128)S(1)} %broadcast_select_fusion), channel_id=1, source_target_pairs={{0,1},{1,2},{2,3},{3,4},{4,5},{5,6},{6,7},{7,8},{8,9},{9,10},{10,1... | collective-permute-start | bytes 3145736 | tf_op jit(solution)/shard_map/ppermute | solution.py:12
  127.8 21.8 %collective-permute-done.18 = f32[512,512]{1,0:T(8,128)S(1)} collective-permute-done((f32[512,512]{1,0:T(8,128)S(1)}, f32[512,512]{1,0:T(8,128)S(1)}, u32[]{:S(2)}, u32[]{:S(2)}) %collective-permute-start.18) | collective-permute-done | bytes 1048608 | tf_op jit(solution)/shard_map/ppermute | solution.py:12
  149.6 0.2 multiply_add_fusion.4
  149.8 2.5 collective-permute-start.19
  152.4 23.4 %collective-permute-done.19 = f32[512,512]{1,0:T(8,128)S(1)} collective-permute-done((f32[512,512]{1,0:T(8,128)S(1)}, f32[512,512]{1,0:T(8,128)S(1)}, u32[]{:S(2)}, u32[]{:S(2)}) %collective-permute-start.19) | collective-permute-done | bytes 1048608 | tf_op jit(solution)/shard_map/ppermute | solution.py:12
  175.8 0.2 multiply_add_fusion.3
  176.0 4.2 %collective-permute-start.20 = (f32[512,512]{1,0:T(8,128)S(1)}, f32[512,512]{1,0:T(8,128)}, u32[]{:S(2)}, u32[]{:S(2)}) collective-permute-start(f32[512,512]{1,0:T(8,128)S(1)} %multiply_add_fusion.3), channel_id=1, source_target_pairs={{0,4},{1,5},{2,6},{3,7},{4,8},{5,9},{6,10},{7,11},{8,12},{9,13},{1... | collective-permute-start | bytes 3145736 | tf_op jit(solution)/shard_map/ppermute | solution.py:12
  180.3 20.7 %collective-permute-done.20 = f32[512,512]{1,0:T(8,128)} collective-permute-done((f32[512,512]{1,0:T(8,128)S(1)}, f32[512,512]{1,0:T(8,128)}, u32[]{:S(2)}, u32[]{:S(2)}) %collective-permute-start.20) | collective-permute-done | bytes 1048608 | tf_op jit(solution)/shard_map/ppermute | solution.py:12
  201.0 0.2 multiply_add_fusion.2
  201.3 29.0 %collective-permute-start.21 = (f32[512,512]{1,0:T(8,128)S(1)}, f32[512,512]{1,0:T(8,128)}, u32[]{:S(2)}, u32[]{:S(2)}) collective-permute-start(f32[512,512]{1,0:T(8,128)S(1)} %multiply_add_fusion.2), channel_id=1, source_target_pairs={{0,8},{1,9},{2,10},{3,11},{4,12},{5,13},{6,14},{7,15},{8,16},{9,17... | collective-permute-start | bytes 3145736 | tf_op jit(solution)/shard_map/ppermute | solution.py:12
  230.3 0.5 copy.46
  231.9 0.3 multiply_add_fusion.1
  232.2 17.7 %collective-permute-start.22 = (f32[512,512]{1,0:T(8,128)S(1)}, f32[512,512]{1,0:T(8,128)S(1)}, u32[]{:S(2)}, u32[]{:S(2)}) collective-permute-start(f32[512,512]{1,0:T(8,128)S(1)} %multiply_add_fusion.1), channel_id=1, source_target_pairs={{0,16},{1,17},{2,18},{3,19},{4,20},{5,21},{6,22},{7,23},{8,24},{9,... | collective-permute-start | bytes 3145736 | tf_op jit(solution)/shard_map/ppermute | solution.py:12
  250.0 1.0 convolution_convert_fusion.1
  251.0 1.3 fusion.90
  252.3 4.6 %fusion = f32[1024,512]{0,1:T(8,128)S(1)} fusion(bf16[512,1024]{1,0:T(8,128)(2,1)S(1)} %copy-done.11, f32[1024,1024]{1,0:T(8,128)S(1)} %fusion.90, f32[1024]{0:T(1024)S(1)} %fusion.4, f32[1024]{0:T(1024)S(1)} %bitcast.74, f32[1024]{0:T(1024)S(1)} %add_bitcast_fusion, s32[1024]{0:T(1024)S(1)} %add_bitcast_fusion.1), kind=kOutput, calls=%fused_computation | convolution fusion | flops 6450839552 | bytes 7356416 | tf_op jit(solution)/shard_map/dot_general | solution.py:122
  256.9 12.7 %collective-permute-done.22 = f32[512,512]{1,0:T(8,128)S(1)} collective-permute-done((f32[512,512]{1,0:T(8,128)S(1)}, f32[512,512]{1,0:T(8,128)S(1)}, u32[]{:S(2)}, u32[]{:S(2)}) %collective-permute-start.22) | collective-permute-done | bytes 1048608 | tf_op jit(solution)/shard_map/ppermute | solution.py:12
  269.7 2.1 fusion.89
  271.8 0.3 multiply_reduce_fusion
  272.1 0.3 copy-done.6
  272.5 0.9 fusion.21
  273.4 1.3 copy.47
  (79 shorter events, 3.0 us)
Async XLA Ops:
  0.0 30.6 %copy-start.2 = (bf16[1024,512]{1,0:T(8,128)(2,1)S(1)}, bf16[1024,512]{1,0:T(8,128)(2,1)}, u32[]{:S(2)}) copy-start(bf16[1024,512]{1,0:T(8,128)(2,1)} %param.9) | copy-start | bytes 3145732
  0.0 26.9 %copy-start.5 = (f32[4,512]{1,0:T(4,128)S(1)}, f32[4,512]{1,0:T(4,128)}, u32[]{:S(2)}) copy-start(f32[4,512]{1,0:T(4,128)} %param.12) | copy-start | bytes 24580
  0.0 26.9 %copy-start.4 = (bf16[3,4,4,128]{3,2,1,0:T(4,128)(2,1)S(1)}, bf16[3,4,4,128]{3,2,1,0:T(4,128)(2,1)}, u32[]{:S(2)}) copy-start(bf16[3,4,4,128]{3,2,1,0:T(4,128)(2,1)} %param.13) | copy-start | bytes 36868
  1.0 91.6 %collective-permute-start.16 = (bf16[3,512]{0,1:T(8,128)(2,1)S(1)}, bf16[3,512]{0,1:T(8,128)(2,1)S(1)}, u32[]{:S(2)}, u32[]{:S(2)}) collective-permute-start(bf16[3,512]{0,1:T(8,128)(2,1)S(1)} %copy.31), channel_id=1, source_target_pairs={{0,1},{1,2},{2,3},{3,4},{4,5},{5,6},{6,7},{7,8},{8,9},{9,10},{10,1... | collective-permute-start | bytes 9224 | tf_op jit(solution)/shard_map/ppermute | solution.py:12
  8.5 24.3 %collective-permute-start = (f32[]{:T(128)}, f32[]{:T(128)}, u32[]{:S(2)}, u32[]{:S(2)}) collective-permute-start(f32[]{:T(128)} %convert_element_type.300), channel_id=1, source_target_pairs={{0,1},{1,2},{2,3},{3,4},{4,5},{5,6},{6,7},{7,8},{8,9},{9,10},{10,1... | collective-permute-start | bytes 20 | tf_op jit(solution)/shard_map/ppermute | solution.py:12
  15.1 27.9 %collective-permute-start.7 = (f32[]{:T(128)}, f32[]{:T(128)}, u32[]{:S(2)}, u32[]{:S(2)}) collective-permute-start(f32[]{:T(128)} %bitcast.5), channel_id=1, source_target_pairs={{0,1},{1,2},{2,3},{3,4},{4,5},{5,6},{6,7},{7,8},{8,9},{9,10},{10,1... | collective-permute-start | bytes 20 | tf_op jit(solution)/shard_map/ppermute | solution.py:12
  21.8 15.8 %collective-permute-start.5 = (f32[]{:T(128)}, f32[]{:T(128)}, u32[]{:S(2)}, u32[]{:S(2)}) collective-permute-start(f32[]{:T(128)} %get-tuple-element.11), channel_id=1, source_target_pairs={{0,1},{1,2},{2,3},{3,4},{4,5},{5,6},{6,7},{7,8},{8,9},{9,10},{10,1... | collective-permute-start | bytes 20 | tf_op jit(solution)/shard_map/ppermute | solution.py:12
  33.5 14.8 %collective-permute-start.1 = (f32[]{:T(128)}, f32[]{:T(128)}, u32[]{:S(2)}, u32[]{:S(2)}) collective-permute-start(f32[]{:T(128)} %select_n.231), channel_id=1, source_target_pairs={{0,1},{1,2},{2,3},{3,4},{4,5},{5,6},{6,7},{7,8},{8,9},{9,10},{10,1... | collective-permute-start | bytes 20 | tf_op jit(solution)/shard_map/ppermute | solution.py:12
  38.2 13.3 %collective-permute-start.6 = (f32[]{:T(128)}, f32[]{:T(128)}, u32[]{:S(2)}, u32[]{:S(2)}) collective-permute-start(f32[]{:T(128)} %select_n.237), channel_id=1, source_target_pairs={{0,1},{1,2},{2,3},{3,4},{4,5},{5,6},{6,7},{7,8},{8,9},{9,10},{10,1... | collective-permute-start | bytes 20 | tf_op jit(solution)/shard_map/ppermute | solution.py:12
  43.6 12.2 %collective-permute-start.9 = (f32[]{:T(128)}, f32[]{:T(128)}, u32[]{:S(2)}, u32[]{:S(2)}) collective-permute-start(f32[]{:T(128)} %select_n.239), channel_id=1, source_target_pairs={{0,1},{1,2},{2,3},{3,4},{4,5},{5,6},{6,7},{7,8},{8,9},{9,10},{10,1... | collective-permute-start | bytes 20 | tf_op jit(solution)/shard_map/ppermute | solution.py:12
  48.9 11.0 %collective-permute-start.2 = (f32[]{:T(128)}, f32[]{:T(128)}, u32[]{:S(2)}, u32[]{:S(2)}) collective-permute-start(f32[]{:T(128)} %max.50), channel_id=1, source_target_pairs={{0,2},{1,3},{2,4},{3,5},{4,6},{5,7},{6,8},{7,9},{8,10},{9,11},{10,... | collective-permute-start | bytes 20 | tf_op jit(solution)/shard_map/ppermute | solution.py:12
  52.2 12.1 %collective-permute-start.8 = (f32[]{:T(128)}, f32[]{:T(128)}, u32[]{:S(2)}, u32[]{:S(2)}) collective-permute-start(f32[]{:T(128)} %max.54), channel_id=1, source_target_pairs={{0,2},{1,3},{2,4},{3,5},{4,6},{5,7},{6,8},{7,9},{8,10},{9,11},{10,... | collective-permute-start | bytes 20 | tf_op jit(solution)/shard_map/ppermute | solution.py:12
  56.3 14.0 %collective-permute-start.11 = (f32[]{:T(128)}, f32[]{:T(128)}, u32[]{:S(2)}, u32[]{:S(2)}) collective-permute-start(f32[]{:T(128)} %add.206), channel_id=1, source_target_pairs={{0,2},{1,3},{2,4},{3,5},{4,6},{5,7},{6,8},{7,9},{8,10},{9,11},{10,... | collective-permute-start | bytes 20 | tf_op jit(solution)/shard_map/ppermute | solution.py:12
  60.6 16.3 %collective-permute-start.3 = (f32[]{:T(128)}, f32[]{:T(128)}, u32[]{:S(2)}, u32[]{:S(2)}) collective-permute-start(f32[]{:T(128)} %max.51), channel_id=1, source_target_pairs={{0,4},{1,5},{2,6},{3,7},{4,8},{5,9},{6,10},{7,11},{8,12},{9,13},{1... | collective-permute-start | bytes 20 | tf_op jit(solution)/shard_map/ppermute | solution.py:12
  64.9 14.9 %collective-permute-start.10 = (f32[]{:T(128)}, f32[]{:T(128)}, u32[]{:S(2)}, u32[]{:S(2)}) collective-permute-start(f32[]{:T(128)} %max.55), channel_id=1, source_target_pairs={{0,4},{1,5},{2,6},{3,7},{4,8},{5,9},{6,10},{7,11},{8,12},{9,13},{1... | collective-permute-start | bytes 20 | tf_op jit(solution)/shard_map/ppermute | solution.py:12
  71.0 11.7 %collective-permute-start.13 = (f32[]{:T(128)}, f32[]{:T(128)}, u32[]{:S(2)}, u32[]{:S(2)}) collective-permute-start(f32[]{:T(128)} %add.208), channel_id=1, source_target_pairs={{0,4},{1,5},{2,6},{3,7},{4,8},{5,9},{6,10},{7,11},{8,12},{9,13},{1... | collective-permute-start | bytes 20 | tf_op jit(solution)/shard_map/ppermute | solution.py:12
  77.6 7.8 %collective-permute-start.4 = (f32[]{:T(128)}, f32[]{:T(128)}, u32[]{:S(2)}, u32[]{:S(2)}) collective-permute-start(f32[]{:T(128)} %max.52), channel_id=1, source_target_pairs={{0,8},{1,9},{2,10},{3,11},{4,12},{5,13},{6,14},{7,15},{8,16},{9,17... | collective-permute-start | bytes 20 | tf_op jit(solution)/shard_map/ppermute | solution.py:12
  80.4 5.6 %collective-permute-start.12 = (f32[]{:T(128)}, f32[]{:T(128)}, u32[]{:S(2)}, u32[]{:S(2)}) collective-permute-start(f32[]{:T(128)} %max.56), channel_id=1, source_target_pairs={{0,8},{1,9},{2,10},{3,11},{4,12},{5,13},{6,14},{7,15},{8,16},{9,17... | collective-permute-start | bytes 20 | tf_op jit(solution)/shard_map/ppermute | solution.py:12
  83.3 6.0 %collective-permute-start.15 = (f32[]{:T(128)}, f32[]{:T(128)}, u32[]{:S(2)}, u32[]{:S(2)}) collective-permute-start(f32[]{:T(128)} %add.210), channel_id=1, source_target_pairs={{0,8},{1,9},{2,10},{3,11},{4,12},{5,13},{6,14},{7,15},{8,16},{9,17... | collective-permute-start | bytes 20 | tf_op jit(solution)/shard_map/ppermute | solution.py:12
  86.7 3.2 %collective-permute-start.14 = (f32[]{:T(128)}, f32[]{:T(128)}, u32[]{:S(2)}, u32[]{:S(2)}) collective-permute-start(f32[]{:T(128)} %max.57), channel_id=1, source_target_pairs={{0,16},{1,17},{2,18},{3,19},{4,20},{5,21},{6,22},{7,23},{8,24},{9,... | collective-permute-start | bytes 20 | tf_op jit(solution)/shard_map/ppermute | solution.py:12
  94.6 1.0 copy-start
  94.7 1.6 copy-start.10
  95.7 27.4 %copy-start.8 = (bf16[1024,512]{1,0:T(8,128)(2,1)}, bf16[1024,512]{1,0:T(8,128)(2,1)S(1)}, u32[]{:S(2)}) copy-start(bf16[1024,512]{1,0:T(8,128)(2,1)S(1)} %multiply_convert_fusion) | copy-start | bytes 3145732
  99.9 23.2 %collective-permute-start.17 = (f32[512,512]{1,0:T(8,128)S(1)}, f32[512,512]{1,0:T(8,128)S(1)}, u32[]{:S(2)}, u32[]{:S(2)}) collective-permute-start(f32[512,512]{1,0:T(8,128)S(1)} %fusion.12), channel_id=1, source_target_pairs={{0,1},{1,2},{2,3},{3,4},{4,5},{5,6},{6,7},{7,8},{8,9},{9,10},{10,1... | collective-permute-start | bytes 3145736 | tf_op jit(solution)/shard_map/ppermute | solution.py:12
  123.2 26.4 %collective-permute-start.18 = (f32[512,512]{1,0:T(8,128)S(1)}, f32[512,512]{1,0:T(8,128)S(1)}, u32[]{:S(2)}, u32[]{:S(2)}) collective-permute-start(f32[512,512]{1,0:T(8,128)S(1)} %broadcast_select_fusion), channel_id=1, source_target_pairs={{0,1},{1,2},{2,3},{3,4},{4,5},{5,6},{6,7},{7,8},{8,9},{9,10},{10,1... | collective-permute-start | bytes 3145736 | tf_op jit(solution)/shard_map/ppermute | solution.py:12
  149.8 26.0 %collective-permute-start.19 = (f32[512,512]{1,0:T(8,128)S(1)}, f32[512,512]{1,0:T(8,128)S(1)}, u32[]{:S(2)}, u32[]{:S(2)}) collective-permute-start(f32[512,512]{1,0:T(8,128)S(1)} %multiply_add_fusion.4), channel_id=1, source_target_pairs={{0,2},{1,3},{2,4},{3,5},{4,6},{5,7},{6,8},{7,9},{8,10},{9,11},{10,... | collective-permute-start | bytes 3145736 | tf_op jit(solution)/shard_map/ppermute | solution.py:12
  176.0 54.3 %copy-start.3 = (bf16[1024,512]{1,0:T(8,128)(2,1)S(1)}, bf16[1024,512]{1,0:T(8,128)(2,1)}, u32[]{:S(2)}) copy-start(bf16[1024,512]{1,0:T(8,128)(2,1)} %param.10) | copy-start | bytes 3145732
  176.0 25.0 %collective-permute-start.20 = (f32[512,512]{1,0:T(8,128)S(1)}, f32[512,512]{1,0:T(8,128)}, u32[]{:S(2)}, u32[]{:S(2)}) collective-permute-start(f32[512,512]{1,0:T(8,128)S(1)} %multiply_add_fusion.3), channel_id=1, source_target_pairs={{0,4},{1,5},{2,6},{3,7},{4,8},{5,9},{6,10},{7,11},{8,12},{9,13},{1... | collective-permute-start | bytes 3145736 | tf_op jit(solution)/shard_map/ppermute | solution.py:12
  201.3 30.7 %collective-permute-start.21 = (f32[512,512]{1,0:T(8,128)S(1)}, f32[512,512]{1,0:T(8,128)}, u32[]{:S(2)}, u32[]{:S(2)}) collective-permute-start(f32[512,512]{1,0:T(8,128)S(1)} %multiply_add_fusion.2), channel_id=1, source_target_pairs={{0,8},{1,9},{2,10},{3,11},{4,12},{5,13},{6,14},{7,15},{8,16},{9,17... | collective-permute-start | bytes 3145736 | tf_op jit(solution)/shard_map/ppermute | solution.py:12
  230.8 19.1 %copy-start.1 = (bf16[1024,512]{0,1:T(8,128)(2,1)S(1)}, bf16[1024,512]{0,1:T(8,128)(2,1)}, u32[]{:S(2)}) copy-start(bf16[1024,512]{0,1:T(8,128)(2,1)} %copy-done) | copy-start | bytes 3145732
  232.2 18.8 %copy-start.9 = (bf16[1024,512]{1,0:T(8,128)(2,1)S(1)}, bf16[1024,512]{1,0:T(8,128)(2,1)}, u32[]{:S(2)}) copy-start(bf16[1024,512]{1,0:T(8,128)(2,1)} %copy-done.8) | copy-start | bytes 3145732
  232.2 37.4 %collective-permute-start.22 = (f32[512,512]{1,0:T(8,128)S(1)}, f32[512,512]{1,0:T(8,128)S(1)}, u32[]{:S(2)}, u32[]{:S(2)}) collective-permute-start(f32[512,512]{1,0:T(8,128)S(1)} %multiply_add_fusion.1), channel_id=1, source_target_pairs={{0,16},{1,17},{2,18},{3,19},{4,20},{5,21},{6,22},{7,23},{8,24},{9,... | collective-permute-start | bytes 3145736 | tf_op jit(solution)/shard_map/ppermute | solution.py:12
  251.0 1.3 copy-start.11
  271.8 0.7 copy-start.6
  271.8 0.7 copy-start.7
where the time goes:
time: 276 us; the launch traced here: 275 us
  starting transfers between devices  124 us (45%)
  waiting for transfers between devices  99.8 us (36%)
  matrix products  15.9 us (6%)
  other arithmetic  13.2 us (5%)
  between operations  11.8 us (4%)
  local copies, waits for them, and re-layouts  9.56 us (3%)
    ppermute x23, starting transfers between devices, passed_along(): return lax.ppermute(shard, axis, pairs)  124 us
    ppermute x23, waiting for transfers between devices, passed_along(): return lax.ppermute(shard, axis, pairs)  99.8 us
  transfers between devices with their start and end apart: 23, of which 5 were waited for; matrix products, arithmetic and copies ran while one was open for 9% of the time, Pallas kernels for 0%

commit v1 on v0

--- a/solution.py
+++ b/solution.py
@@ -4,6 +4,8 @@
 from jax.sharding import PartitionSpec as P
 
 HIGHEST = lax.Precision.HIGHEST
+AXES = ("outer", "inner")
+PAD_ROWS = 8
 
 
 def passed_along(shard, axis, by):
@@ -37,30 +39,45 @@
     return (new_memory, new_level, decay_first + decay_second, jnp.maximum(cut_first, cut_second))
 
 
-def prefix_before(state, identity, count, token_position, mover):
-    distances = [1]
-    reach = 1
-    while reach < count - 1:
-        distances.append(reach)
-        reach = reach * 2
-    current = state
-    for step_number, distance in enumerate(distances):
-        arrived = mover(current, distance)
-        present = token_position >= distance
-        arrived = tuple(
-            (jnp.where(present, piece, blank) for piece, blank in zip(arrived, identity))
+def pack(state):
+    memory, level, decay, cut = state
+    channels = memory.shape[1]
+    lane = jnp.arange(channels)[None, :]
+    row = jnp.where(lane == 0, level, jnp.where(lane == 1, decay, jnp.where(lane == 2, cut, 0.0)))
+    extra = jnp.concatenate([row, jnp.zeros((PAD_ROWS - 1, channels), jnp.float32)], axis=0)
+    return jnp.concatenate([memory, extra], axis=0)
+
+
+def unpack(message, rows):
+    return message[:rows], message[rows, 0], message[rows, 1], message[rows, 2]
+
+
+def exclusive_prefix(own_state, me, count):
+    rows = own_state[0].shape[0]
+    inclusive = own_state
+    exclusive = None
+    distance = 1
+    while distance < count:
+        arrived = unpack(passed_along(pack(inclusive), AXES, distance), rows)
+        present = me >= distance
+        memory, level, decay, cut = arrived
+        arrived = (
+            memory,
+            jnp.where(present, level, -jnp.inf),
+            jnp.where(present, decay, 0.0),
+            jnp.where(present, cut, 0.0),
         )
-        if step_number == 0:
-            current = arrived
-        else:
-            current = combine(arrived, current)
-    return current
+        exclusive = arrived if exclusive is None else combine(arrived, exclusive)
+        if 2 * distance < count:
+            inclusive = combine(arrived, inclusive)
+        distance *= 2
+    return exclusive
 
 
 def body(token_ids, inner_x, out_gate, gate_pre, conv_weight, qkv_weight, norm_gain, skip_gain):
     num_rows, channels = inner_x.shape
     kernel_taps = conv_weight.shape[0]
-    rim_rows = passed_along(inner_x[num_rows - kernel_taps + 1 :], ("outer", "inner"), 1)
+    rim_rows = passed_along(inner_x[num_rows - kernel_taps + 1 :], AXES, 1)
     extended = jnp.concatenate([rim_rows, inner_x], axis=0)
     conv_sum = jnp.zeros((num_rows, channels), jnp.float32)
     for offset in range(kernel_taps):
@@ -94,19 +111,7 @@
         weighted_keys, value_float, (((0,), (0,)), ((), ())), precision=HIGHEST
     )
     own_state = (summary, tail_level, log_decay[num_rows - 1], (last_mark > 0).astype(jnp.float32))
-    identity = (
-        jnp.zeros_like(summary),
-        jnp.array(-jnp.inf, jnp.float32),
-        jnp.array(0.0, jnp.float32),
-        jnp.array(0.0, jnp.float32),
-    )
-    incoming = prefix_before(
-        own_state,
-        identity,
-        lax.axis_size(("outer", "inner")),
-        lax.axis_index(("outer", "inner")),
-        lambda state, distance: passed_along(state, ("outer", "inner"), distance),
-    )
+    incoming = exclusive_prefix(own_state, lax.axis_index(AXES), lax.axis_size(AXES))
     token_position = jnp.arange(num_rows)
     valid = (token_position[None, :] <= token_position[:, None]) & (
         doc_marks[None, :] == doc_marks[:, None]
@@ -142,15 +147,15 @@
         body,
         mesh=mesh,
         in_specs=(
-            P(("outer", "inner")),
-            P(("outer", "inner"), None),
-            P(("outer", "inner"), None),
-            P(None, ("outer", "inner")),
+            P(AXES),
+            P(AXES, None),
+            P(AXES, None),
+            P(None, AXES),
             P(),
             P(),
             P(),
             P(),
         ),
-        out_specs=P(("outer", "inner"), None),
+        out_specs=P(AXES, None),
         check_vma=False,
     )

time: 276 us -> 215 us (0.78)
  starting transfers between devices: 124 us -> 63.3 us
  waiting for transfers between devices: 99.8 us -> 74.3 us
  local copies, waits for them, and re-layouts: 9.56 us -> 19.4 us
  other arithmetic: 13.2 us -> 21.8 us
  matrix products: 15.9 us -> 23 us
    ppermute x23 -> x6, starting transfers between devices: 124 us -> 63.3 us  [passed_along(): return lax.ppermute(shard, axis, pairs)]
    ppermute x23 -> x6, waiting for transfers between devices: 99.8 us -> 74.3 us  [passed_along(): return lax.ppermute(shard, axis, pairs)]
    slice x3 -> x8, local copies, waits for them, and re-layouts: 1.04 us -> 7.83 us  [the longest x5 6.87 us: unpack(): message[rows, 0]]
    add x4, other arithmetic: 0.98 us -> 5.84 us  [combine(): jnp.exp(kept_level - safe_level) * memory_first]
    dot_general x1, matrix products: 2.11 us -> 5.86 us  [body(): jnp.dot(query_rows.astype(jnp.float32), incoming[0], precision=HIGHEST)]
  transfers between devices with their start and end apart: 23 -> 6, of which waited for: 5 -> 4; matrix products, arithmetic and copies ran while one was open for 9% -> 14% of each run, Pallas kernels for 0% -> 0%
where the time goes in v1:
time: 215 us; the launch traced here: 214 us
  waiting for transfers between devices  74.3 us (35%)
  starting transfers between devices  63.3 us (29%)
  matrix products  23 us (11%)
  other arithmetic  21.8 us (10%)
  local copies, waits for them, and re-layouts  19.4 us (9%)
  between operations  12.5 us (6%)
    ppermute x6, waiting for transfers between devices, passed_along(): return lax.ppermute(shard, axis, pairs)  74.3 us
    ppermute x6, starting transfers between devices, passed_along(): return lax.ppermute(shard, axis, pairs)  63.3 us
    slice x5, local copies, waits for them, and re-layouts, unpack(): message[rows, 0]  6.87 us
    dot_general x1, matrix products, body(): local_sum = jnp.dot(weights, value_float, precision=HIGHEST)  6.67 us
    dot_general x1, matrix products, body(): jnp.dot(query_rows.astype(jnp.float32), incoming[0], precision=HIGHEST)  5.86 us
    add x4, other arithmetic, combine(): jnp.exp(kept_level - safe_level) * memory_first  5.84 us
    unnamed x18, local copies, waits for them, and re-layouts  4.43 us
  transfers between devices with their start and end apart: 6, of which 4 were waited for; matrix products, arithmetic and copies ran while one was open for 14% of the time, Pallas kernels for 0%

profile of v1, /device:TPU:0, one launch (start us, length us, event | category | flops | bytes accessed | tf_op | source)
XLA Modules:
  0.0 214.3 jit_solution(12442979488657033352)
XLA Ops:
  0.0 0.7 slice.159
  0.7 0.2 copy.31
  0.9 4.8 %collective-permute-start = (bf16[3,512]{0,1:T(8,128)(2,1)S(1)}, bf16[3,512]{0,1:T(8,128)(2,1)S(1)}, u32[]{:S(2)}, u32[]{:S(2)}) collective-permute-start(bf16[3,512]{0,1:T(8,128)(2,1)S(1)} %copy.31), channel_id=1, source_target_pairs={{0,1},{1,2},{2,3},{3,4},{4,5},{5,6},{6,7},{7,8},{8,9},{9,10},{10,1... | collective-permute-start | bytes 9224 | tf_op jit(solution)/shard_map/ppermute | solution.py:14
  5.8 0.7 convert_bitcast_fusion
  6.5 0.3 reduce-window.16
  6.9 0.1 slice_reduce_fusion.1
  7.0 0.6 slice.155
  7.6 0.7 compare_bitcast_fusion
  9.0 0.9 fusion.107
  9.9 0.7 slice_bitcast_fusion.2
  10.6 0.1 copy.41
  10.8 0.1 copy.40
  11.3 0.1 copy.38
  11.5 0.7 slice_negate_fusion
  12.2 0.3 reduce-window.24
  12.6 0.1 slice_reduce_fusion
  12.8 0.7 slice.156
  13.5 0.8 add_subtract_fusion
  14.3 1.3 fusion.95
  15.6 1.9 subtract_exponential_fusion
  17.5 3.5 %convolution_convert_fusion.1 = bf16[512,1024]{1,0:T(8,128)(2,1)} fusion(bf16[1024,512]{1,0:T(8,128)(2,1)} %param.9, f32[512]{0:T(512)S(1)} %reshape.515, f32[512]{0:T(512)S(1)} %reshape.514, f32[512]{0:T(512)S(1)} %reshape.513, f32[512]{0:T(512)S(1)} %reshape.512, f32[512]{0:T(512)S(1)} %get-tuple-element.46, f32[512]{0:T(512)S(1)} %get-tuple-element.47, ...), kind=kOutput, calls=%fused_computation.35 | convolution fusion | flops 540016640 | bytes 2115584 | tf_op jit(solution)/shard_map/dot_general | solution.py:97
  21.0 1.3 select_select_fusion.4
  22.2 0.5 copy.32
  22.8 0.1 copy.37
  23.0 0.1 copy.36
  23.2 0.1 copy.35
  23.8 2.1 multiply_convert_fusion.1
  25.8 1.0 multiply_convert_fusion
  26.9 1.0 copy-done.4
  27.9 3.7 %fusion.17 = f32[512,512]{1,0:T(8,128)S(1)} fusion(bf16[512,1024]{1,0:T(8,128)(2,1)S(1)} %copy-done.6, bf16[1024,512]{1,0:T(8,128)(2,1)S(1)} %multiply_convert_fusion, f32[1024]{0:T(1024)S(1)} %subtract_exponential_fusion), kind=kOutput, calls=%fused_computation.22 | convolution fusion | flops 3222274048 | bytes 3149824 | tf_op jit(solution)/shard_map/dot_general | solution.py:110
  31.5 0.1 maximum_maximum_fusion
  31.7 4.5 %collective-permute-start.1 = (f32[520,512]{1,0:T(8,128)S(1)}, f32[520,512]{1,0:T(8,128)}, u32[]{:S(2)}, u32[]{:S(2)}) collective-permute-start(f32[520,512]{1,0:T(8,128)S(1)} %maximum_maximum_fusion), channel_id=1, source_target_pairs={{0,1},{1,2},{2,3},{3,4},{4,5},{5,6},{6,7},{7,8},{8,9},{9,10},{10,1... | collective-permute-start | bytes 3194888 | tf_op jit(solution)/shard_map/ppermute | solution.py:14
  36.1 21.5 %collective-permute-done.1 = f32[520,512]{1,0:T(8,128)} collective-permute-done((f32[520,512]{1,0:T(8,128)S(1)}, f32[520,512]{1,0:T(8,128)}, u32[]{:S(2)}, u32[]{:S(2)}) %collective-permute-start.1) | collective-permute-done | bytes 1064992 | tf_op jit(solution)/shard_map/ppermute | solution.py:14
  57.6 1.4 fusion.106
  63.5 1.5 multiply_add_fusion.4
  65.0 1.1 maximum_maximum_fusion.1
  66.1 6.4 %collective-permute-start.2 = (f32[520,512]{1,0:T(8,128)}, f32[520,512]{1,0:T(8,128)}, u32[]{:S(2)}, u32[]{:S(2)}) collective-permute-start(f32[520,512]{1,0:T(8,128)} %maximum_maximum_fusion.1), channel_id=1, source_target_pairs={{0,2},{1,3},{2,4},{3,5},{4,6},{5,7},{6,8},{7,9},{8,10},{9,11},{10,... | collective-permute-start | bytes 3194888 | tf_op jit(solution)/shard_map/ppermute | solution.py:14
  72.5 21.9 %collective-permute-done.2 = f32[520,512]{1,0:T(8,128)} collective-permute-done((f32[520,512]{1,0:T(8,128)}, f32[520,512]{1,0:T(8,128)}, u32[]{:S(2)}, u32[]{:S(2)}) %collective-permute-start.2) | collective-permute-done | bytes 1064992 | tf_op jit(solution)/shard_map/ppermute | solution.py:14
  94.4 1.4 fusion.105
  97.8 1.5 multiply_add_fusion.3
  99.3 0.1 maximum_maximum_fusion.2
  99.4 5.4 %collective-permute-start.3 = (f32[520,512]{1,0:T(8,128)S(1)}, f32[520,512]{1,0:T(8,128)}, u32[]{:S(2)}, u32[]{:S(2)}) collective-permute-start(f32[520,512]{1,0:T(8,128)S(1)} %maximum_maximum_fusion.2), channel_id=1, source_target_pairs={{0,4},{1,5},{2,6},{3,7},{4,8},{5,9},{6,10},{7,11},{8,12},{9,13},{1... | collective-permute-start | bytes 3194888 | tf_op jit(solution)/shard_map/ppermute | solution.py:14
  104.8 22.0 %collective-permute-done.3 = f32[520,512]{1,0:T(8,128)} collective-permute-done((f32[520,512]{1,0:T(8,128)S(1)}, f32[520,512]{1,0:T(8,128)}, u32[]{:S(2)}, u32[]{:S(2)}) %collective-permute-start.3) | collective-permute-done | bytes 1064992 | tf_op jit(solution)/shard_map/ppermute | solution.py:14
  126.8 1.4 fusion.104
  130.2 1.5 multiply_add_fusion.2
  131.7 1.1 maximum_maximum_fusion.3
  132.8 28.0 %collective-permute-start.4 = (f32[520,512]{1,0:T(8,128)}, f32[520,512]{1,0:T(8,128)}, u32[]{:S(2)}, u32[]{:S(2)}) collective-permute-start(f32[520,512]{1,0:T(8,128)} %maximum_maximum_fusion.3), channel_id=1, source_target_pairs={{0,8},{1,9},{2,10},{3,11},{4,12},{5,13},{6,14},{7,15},{8,16},{9,17... | collective-permute-start | bytes 3194888 | tf_op jit(solution)/shard_map/ppermute | solution.py:14
  160.7 1.5 copy.46
  163.1 1.8 fusion.4
  165.0 1.4 fusion.103
  168.4 1.5 multiply_add_fusion.1
  169.9 0.1 maximum_maximum_fusion.4
  170.0 14.2 %collective-permute-start.5 = (f32[520,512]{1,0:T(8,128)S(1)}, f32[520,512]{1,0:T(8,128)}, u32[]{:S(2)}, u32[]{:S(2)}) collective-permute-start(f32[520,512]{1,0:T(8,128)S(1)} %maximum_maximum_fusion.4), channel_id=1, source_target_pairs={{0,16},{1,17},{2,18},{3,19},{4,20},{5,21},{6,22},{7,23},{8,24},{9,... | collective-permute-start | bytes 3194888 | tf_op jit(solution)/shard_map/ppermute | solution.py:14
  184.3 1.0 convolution_convert_fusion
  185.3 1.0 copy-done.1
  186.3 1.3 fusion.109
  187.6 6.7 %fusion = f32[1024,512]{0,1:T(8,128)} fusion(bf16[512,1024]{1,0:T(8,128)(2,1)S(1)} %copy-done.7, f32[1024,1024]{1,0:T(8,128)S(1)} %fusion.109, f32[1024]{0:T(1024)S(1)} %fusion.4, f32[1024]{0:T(1024)S(1)} %bitcast.88, f32[1024]{0:T(1024)S(1)} %add_bitcast_fusion, s32[1024]{0:T(1024)S(1)} %add_bitcast_fusion.1), kind=kOutput, calls=%fused_computation | convolution fusion | flops 6450839552 | bytes 7356416 | tf_op jit(solution)/shard_map/dot_general | solution.py:127
  194.6 8.9 %collective-permute-done.5 = f32[520,512]{1,0:T(8,128)} collective-permute-done((f32[520,512]{1,0:T(8,128)S(1)}, f32[520,512]{1,0:T(8,128)}, u32[]{:S(2)}, u32[]{:S(2)}) %collective-permute-start.5) | collective-permute-done | bytes 1064992 | tf_op jit(solution)/shard_map/ppermute | solution.py:14
  203.5 1.2 slice.229
  205.5 5.9 %fusion.108 = (f32[1024]{0:T(1024)S(1)}, f32[1024,512]{0,1:T(8,128)S(1)}) fusion(f32[1024,512]{0,1:T(8,128)} %fusion, f32[1024]{0:T(1024)S(1)} %get-tuple-element.18, bf16[1024,512]{1,0:T(8,128)(2,1)} %copy-done.1, f32[520,512]{1,0:T(8,128)} %collective-permute-done.5, f32[520,512]{1,0:T(8,128)} %collective-permute-done.4, ...), kind=kOutput, calls=%fused_computation.178 | convolution fusion | flops 3226467328 | bytes 10498080 | tf_op jit(solution)/shard_map/dot_general | solution.py:130
  211.4 0.3 multiply_reduce_fusion
  211.7 0.3 copy-done.2
  212.0 0.9 fusion.21
  213.0 1.3 copy.47
  (54 shorter events, 2.5 us)
Async XLA Ops:
  0.9 22.9 %collective-permute-start = (bf16[3,512]{0,1:T(8,128)(2,1)S(1)}, bf16[3,512]{0,1:T(8,128)(2,1)S(1)}, u32[]{:S(2)}, u32[]{:S(2)}) collective-permute-start(bf16[3,512]{0,1:T(8,128)(2,1)S(1)} %copy.31), channel_id=1, source_target_pairs={{0,1},{1,2},{2,3},{3,4},{4,5},{5,6},{6,7},{7,8},{8,9},{9,10},{10,1... | collective-permute-start | bytes 9224 | tf_op jit(solution)/shard_map/ppermute | solution.py:14
  17.5 4.8 %copy-start = (bf16[1024,512]{1,0:T(8,128)(2,1)S(1)}, bf16[1024,512]{1,0:T(8,128)(2,1)}, u32[]{:S(2)}) copy-start(bf16[1024,512]{1,0:T(8,128)(2,1)} %param.9) | copy-start | bytes 3145732
  25.8 2.0 copy-start.6
  26.9 1.0 copy-start.4
  31.7 25.9 %collective-permute-start.1 = (f32[520,512]{1,0:T(8,128)S(1)}, f32[520,512]{1,0:T(8,128)}, u32[]{:S(2)}, u32[]{:S(2)}) collective-permute-start(f32[520,512]{1,0:T(8,128)S(1)} %maximum_maximum_fusion), channel_id=1, source_target_pairs={{0,1},{1,2},{2,3},{3,4},{4,5},{5,6},{6,7},{7,8},{8,9},{9,10},{10,1... | collective-permute-start | bytes 3194888 | tf_op jit(solution)/shard_map/ppermute | solution.py:14
  66.1 28.3 %collective-permute-start.2 = (f32[520,512]{1,0:T(8,128)}, f32[520,512]{1,0:T(8,128)}, u32[]{:S(2)}, u32[]{:S(2)}) collective-permute-start(f32[520,512]{1,0:T(8,128)} %maximum_maximum_fusion.1), channel_id=1, source_target_pairs={{0,2},{1,3},{2,4},{3,5},{4,6},{5,7},{6,8},{7,9},{8,10},{9,11},{10,... | collective-permute-start | bytes 3194888 | tf_op jit(solution)/shard_map/ppermute | solution.py:14
  99.4 27.3 %collective-permute-start.3 = (f32[520,512]{1,0:T(8,128)S(1)}, f32[520,512]{1,0:T(8,128)}, u32[]{:S(2)}, u32[]{:S(2)}) collective-permute-start(f32[520,512]{1,0:T(8,128)S(1)} %maximum_maximum_fusion.2), channel_id=1, source_target_pairs={{0,4},{1,5},{2,6},{3,7},{4,8},{5,9},{6,10},{7,11},{8,12},{9,13},{1... | collective-permute-start | bytes 3194888 | tf_op jit(solution)/shard_map/ppermute | solution.py:14
  132.8 32.2 %collective-permute-start.4 = (f32[520,512]{1,0:T(8,128)}, f32[520,512]{1,0:T(8,128)}, u32[]{:S(2)}, u32[]{:S(2)}) collective-permute-start(f32[520,512]{1,0:T(8,128)} %maximum_maximum_fusion.3), channel_id=1, source_target_pairs={{0,8},{1,9},{2,10},{3,11},{4,12},{5,13},{6,14},{7,15},{8,16},{9,17... | collective-permute-start | bytes 3194888 | tf_op jit(solution)/shard_map/ppermute | solution.py:14
  170.0 16.3 %copy-start.5 = (bf16[1024,512]{1,0:T(8,128)(2,1)S(1)}, bf16[1024,512]{1,0:T(8,128)(2,1)}, u32[]{:S(2)}) copy-start(bf16[1024,512]{1,0:T(8,128)(2,1)} %copy-done.4) | copy-start | bytes 3145732
  170.0 33.5 %collective-permute-start.5 = (f32[520,512]{1,0:T(8,128)S(1)}, f32[520,512]{1,0:T(8,128)}, u32[]{:S(2)}, u32[]{:S(2)}) collective-permute-start(f32[520,512]{1,0:T(8,128)S(1)} %maximum_maximum_fusion.4), channel_id=1, source_target_pairs={{0,16},{1,17},{2,18},{3,19},{4,20},{5,21},{6,22},{7,23},{8,24},{9,... | collective-permute-start | bytes 3194888 | tf_op jit(solution)/shard_map/ppermute | solution.py:14
  185.3 1.0 copy-start.1
  186.3 1.3 copy-start.7
  211.3 0.7 copy-start.2
  211.4 0.7 copy-start.3

commit v2 on v1

--- a/solution.py
+++ b/solution.py
@@ -6,6 +6,7 @@
 HIGHEST = lax.Precision.HIGHEST
 AXES = ("outer", "inner")
 PAD_ROWS = 8
+MESSAGE_DTYPE = jnp.float32
 
 
 def passed_along(shard, axis, by):
@@ -26,6 +27,25 @@
     return jnp.where(same_block, dense_matrix, 0.0).astype(block_table.dtype)
 
 
+def split_bf16(values):
+    high = lax.reduce_precision(values, exponent_bits=8, mantissa_bits=7)
+    return high.astype(jnp.bfloat16), (values - high).astype(jnp.bfloat16)
+
+
+def dot_two_pass(left, right, dims):
+    high, low = split_bf16(left)
+    first = lax.dot_general(high, right, dims, preferred_element_type=jnp.float32)
+    return first + lax.dot_general(low, right, dims, preferred_element_type=jnp.float32)
+
+
+def dot_any(left, right_message, dims):
+    if right_message.dtype == jnp.bfloat16:
+        return lax.dot_general(left, right_message, dims, preferred_element_type=jnp.float32)
+    high, low = split_bf16(right_message)
+    first = lax.dot_general(left, high, dims, preferred_element_type=jnp.float32)
+    return first + lax.dot_general(left, low, dims, preferred_element_type=jnp.float32)
+
+
 def combine(earlier, later):
     memory_first, level_first, decay_first, cut_first = earlier
     memory_second, level_second, decay_second, cut_second = later
@@ -43,35 +63,64 @@
     memory, level, decay, cut = state
     channels = memory.shape[1]
     lane = jnp.arange(channels)[None, :]
-    row = jnp.where(lane == 0, level, jnp.where(lane == 1, decay, jnp.where(lane == 2, cut, 0.0)))
-    extra = jnp.concatenate([row, jnp.zeros((PAD_ROWS - 1, channels), jnp.float32)], axis=0)
-    return jnp.concatenate([memory, extra], axis=0)
+    scalars = [level, decay, cut]
+    if MESSAGE_DTYPE == jnp.bfloat16:
+        parts = []
+        for value in scalars:
+            high = lax.reduce_precision(value, exponent_bits=8, mantissa_bits=7)
+            rest = value - high
+            middle = lax.reduce_precision(rest, exponent_bits=8, mantissa_bits=7)
+            parts.append((high, middle, rest - middle))
+        rows = [
+            sum(jnp.where(lane == index, parts[index][piece], 0.0) for index in range(3))
+            for piece in range(3)
+        ]
+    else:
+        rows = [sum(jnp.where(lane == index, scalars[index], 0.0) for index in range(3))]
+    pad_rows = PAD_ROWS - len(rows)
+    extra = jnp.concatenate(rows + [jnp.zeros((pad_rows, channels), jnp.float32)], axis=0)
+    return jnp.concatenate([memory.astype(MESSAGE_DTYPE), extra.astype(MESSAGE_DTYPE)], axis=0)
 
 
 def unpack(message, rows):
-    return message[:rows], message[rows, 0], message[rows, 1], message[rows, 2]
-
-
-def exclusive_prefix(own_state, me, count):
+    if MESSAGE_DTYPE == jnp.bfloat16:
+        tail = message[rows : rows + 3, :3].astype(jnp.float32)
+        scalars = (tail[0] + tail[1]) + tail[2]
+    else:
+        scalars = message[rows, :3]
+    return message[:rows], scalars[0], scalars[1], scalars[2]
+
+
+def scan_and_read(own_state, me, count, query_rows, local_parts):
     rows = own_state[0].shape[0]
     inclusive = own_state
-    exclusive = None
+    earlier = None
+    total = None
     distance = 1
     while distance < count:
-        arrived = unpack(passed_along(pack(inclusive), AXES, distance), rows)
+        message = passed_along(pack(inclusive), AXES, distance)
+        if earlier is None:
+            message, local_parts = lax.optimization_barrier((message, local_parts))
+        memory, level, decay, cut = unpack(message, rows)
         present = me >= distance
-        memory, level, decay, cut = arrived
-        arrived = (
-            memory,
-            jnp.where(present, level, -jnp.inf),
-            jnp.where(present, decay, 0.0),
-            jnp.where(present, cut, 0.0),
-        )
-        exclusive = arrived if exclusive is None else combine(arrived, exclusive)
+        level = jnp.where(present, level, -jnp.inf)
+        decay = jnp.where(present, decay, 0.0)
+        cut = jnp.where(present, cut, 0.0)
+        term = dot_any(query_rows, memory, (((1,), (0,)), ((), ())))
+        if earlier is None:
+            earlier = (level, decay, cut)
+            total = term
+        else:
+            level_later, decay_later, cut_later = earlier
+            kept_level = jnp.where(cut_later > 0.5, -jnp.inf, level + decay_later)
+            new_level = jnp.maximum(kept_level, level_later)
+            safe_level = jnp.where(new_level == -jnp.inf, 0.0, new_level)
+            total = jnp.exp(kept_level - safe_level) * term + jnp.exp(level_later - safe_level) * total
+            earlier = (new_level, decay + decay_later, jnp.maximum(cut, cut_later))
         if 2 * distance < count:
-            inclusive = combine(arrived, inclusive)
+            inclusive = combine((memory.astype(jnp.float32), level, decay, cut), inclusive)
         distance *= 2
-    return exclusive
+    return total, earlier[0], local_parts
 
 
 def body(token_ids, inner_x, out_gate, gate_pre, conv_weight, qkv_weight, norm_gain, skip_gain):
@@ -101,17 +150,13 @@
     log_decay = jnp.cumsum(jax.nn.log_sigmoid(gate_pre[1]))
     doc_marks = jnp.cumsum((token_ids == 0).astype(jnp.int32))
     last_mark = doc_marks[num_rows - 1]
-    value_float = value_rows.astype(jnp.float32)
     tail_weight = jnp.where(
         doc_marks == last_mark, log_decay[num_rows - 1] - log_decay + input_gate, -jnp.inf
     )
     tail_level = jnp.max(tail_weight)
     weighted_keys = jnp.exp(tail_weight - tail_level)[:, None] * key_rows.astype(jnp.float32)
-    summary = lax.dot_general(
-        weighted_keys, value_float, (((0,), (0,)), ((), ())), precision=HIGHEST
-    )
+    summary = dot_two_pass(weighted_keys, value_rows, (((0,), (0,)), ((), ())))
     own_state = (summary, tail_level, log_decay[num_rows - 1], (last_mark > 0).astype(jnp.float32))
-    incoming = exclusive_prefix(own_state, lax.axis_index(AXES), lax.axis_size(AXES))
     token_position = jnp.arange(num_rows)
     valid = (token_position[None, :] <= token_position[:, None]) & (
         doc_marks[None, :] == doc_marks[:, None]
@@ -124,10 +169,12 @@
         query_rows, key_rows, (((1,), (1,)), ((), ())), preferred_element_type=jnp.float32
     )
     weights = jnp.exp(log_weight - local_max[:, None]) * scores
-    local_sum = jnp.dot(weights, value_float, precision=HIGHEST)
-    carried = jnp.where(doc_marks == 0, log_decay + incoming[1], -jnp.inf)
+    local_sum = dot_two_pass(weights, value_rows, (((1,), (0,)), ((), ())))
+    from_memory, incoming_level, (local_sum, local_max) = scan_and_read(
+        own_state, lax.axis_index(AXES), lax.axis_size(AXES), query_rows, (local_sum, local_max)
+    )
+    carried = jnp.where(doc_marks == 0, log_decay + incoming_level, -jnp.inf)
     row_max = jnp.maximum(carried, local_max)
-    from_memory = jnp.dot(query_rows.astype(jnp.float32), incoming[0], precision=HIGHEST)
     retrieved = (
         jnp.exp(carried - row_max)[:, None] * from_memory
         + jnp.exp(local_max - row_max)[:, None] * local_sum

time: 215 us -> 220 us (1.023)
  matrix products: 23 us -> 38.5 us
  starting transfers between devices: 63.3 us -> 55.8 us
  other arithmetic: 21.8 us -> 29.2 us
  waiting for transfers between devices: 74.3 us -> 67.5 us
  local copies, waits for them, and re-layouts: 19.4 us -> 14.6 us
    dot_general x3 -> x14, matrix products: 16.2 us -> 32.6 us  [the longest x5 14 us: dot_any(): lax.dot_general(left, low, dims, preferred_element_type=jnp.float32)]
    ppermute x6, starting transfers between devices: 63.3 us -> 55.8 us  [passed_along(): return lax.ppermute(shard, axis, pairs)]
    ppermute x6, waiting for transfers between devices: 74.3 us -> 67.5 us  [passed_along(): return lax.ppermute(shard, axis, pairs)]
    reduce_sum x0 -> x1, other arithmetic: none -> 4.81 us  [body(): average = jnp.mean(retrieved, axis=1, keepdims=True)]
    unnamed x18 -> x32, local copies, waits for them, and re-layouts: 4.43 us -> 1.62 us
  transfers between devices with their start and end apart: 6 -> 6, of which waited for: 4 -> 4; matrix products, arithmetic and copies ran while one was open for 14% -> 22% of each run, Pallas kernels for 0% -> 0%
where the time goes in v2:
time: 220 us; the launch traced here: 218 us
  waiting for transfers between devices  67.5 us (31%)
  starting transfers between devices  55.8 us (25%)
  matrix products  38.5 us (18%)
  other arithmetic  29.2 us (13%)
  local copies, waits for them, and re-layouts  14.6 us (7%)
  between operations  12.7 us (6%)
    ppermute x6, waiting for transfers between devices, passed_along(): return lax.ppermute(shard, axis, pairs)  67.5 us
    ppermute x6, starting transfers between devices, passed_along(): return lax.ppermute(shard, axis, pairs)  55.8 us
    dot_general x5, matrix products, dot_any(): lax.dot_general(left, low, dims, preferred_element_type=jnp.float32)  14 us
    dot_general x5, matrix products, dot_any(): lax.dot_general(left, high, dims, preferred_element_type=jnp.float32)  12.6 us
    slice x5, local copies, waits for them, and re-layouts, unpack(): return (message[:rows], scalars[0], scalars[1], scalars[2])  6.33 us
    add x4, other arithmetic, combine(): jnp.exp(kept_level - safe_level) * memory_first  5.92 us
    reduce_sum x1, other arithmetic, body(): average = jnp.mean(retrieved, axis=1, keepdims=True)  4.81 us
    concatenate x5, other arithmetic, pack(): jnp.concatenate([memory.astype(MESSAGE_DTYPE), extra.astype(MESSAGE_DTYPE...  4.69 us
  transfers between devices with their start and end apart: 6, of which 4 were waited for; matrix products, arithmetic and copies ran while one was open for 22% of the time, Pallas kernels for 0%

profile of v2, /device:TPU:0, one launch (start us, length us, event | category | flops | bytes accessed | tf_op | source)
XLA Modules:
  0.0 218.3 jit_solution(16958780054279351442)
XLA Ops:
  0.0 0.7 slice.190
  0.7 4.8 %collective-permute-start = (bf16[3,512]{1,0:T(4,128)(2,1)S(1)}, bf16[3,512]{1,0:T(4,128)(2,1)S(1)}, u32[]{:S(2)}, u32[]{:S(2)}) collective-permute-start(bf16[3,512]{1,0:T(4,128)(2,1)S(1)} %slice.190), channel_id=1, source_target_pairs={{0,1},{1,2},{2,3},{3,4},{4,5},{5,6},{6,7},{7,8},{8,9},{9,10},{10,1... | collective-permute-start | bytes 9224 | tf_op jit(solution)/shard_map/ppermute | solution.py:15
  5.6 0.7 convert_bitcast_fusion
  6.2 0.3 reduce-window.16
  6.8 0.6 slice.186
  8.1 0.7 compare_bitcast_fusion
  8.8 0.7 slice_negate_fusion
  9.5 0.3 reduce-window.24
  10.1 0.7 slice.187
  10.8 0.7 add_subtract_fusion
  11.5 1.3 fusion.99
  12.8 1.8 fusion.1
  14.6 1.9 subtract_exponential_fusion
  16.5 0.9 fusion.100
  17.4 0.7 slice_bitcast_fusion
  19.1 2.5 %convolution_convert_fusion.1 = bf16[512,1024]{1,0:T(8,128)(2,1)S(1)} fusion(bf16[1024,512]{1,0:T(8,128)(2,1)} %param.9, f32[512]{0:T(512)S(1)} %reshape.547, f32[512]{0:T(512)S(1)} %reshape.546, f32[512]{0:T(512)S(1)} %reshape.545, f32[512]{0:T(512)S(1)} %reshape.544, f32[512]{0:T(512)S(1)} %get-tuple-element.52, f32[512]{0:T(512)S(1)} %get-tuple-element.53, ...), kind=kOutput, calls=%fused_computation.40 | convolution fusion | flops 540016640 | bytes 2115584 | tf_op jit(solution)/shard_map/dot_general | solution.py:146
  21.6 1.2 select_add_fusion.4
  24.7 1.4 multiply_convert_fusion.1
  26.2 0.9 multiply_convert_fusion
  27.1 1.0 fusion.26
  28.2 1.1 convolution_add_fusion
  29.2 0.1 maximum_maximum_fusion
  29.4 3.7 %collective-permute-start.1 = (f32[520,512]{1,0:T(8,128)S(1)}, f32[520,512]{1,0:T(8,128)S(1)}, u32[]{:S(2)}, u32[]{:S(2)}) collective-permute-start(f32[520,512]{1,0:T(8,128)S(1)} %maximum_maximum_fusion), channel_id=1, source_target_pairs={{0,1},{1,2},{2,3},{3,4},{4,5},{5,6},{6,7},{7,8},{8,9},{9,10},{10,1... | collective-permute-start | bytes 3194888 | tf_op jit(solution)/shard_map/ppermute | solution.py:15
  33.1 0.9 convolution_convert_fusion
  34.1 1.6 exponential_multiply_fusion
  35.6 1.3 fusion.10
  36.9 2.6 %fusion.12 = f32[1024,512]{1,0:T(8,128)} fusion(f32[1024,512]{1,0:T(8,128)S(1)} %fusion.10, bf16[512,1024]{1,0:T(8,128)(2,1)S(1)} %copy-done.12, f32[1024,1024]{1,0:T(8,128)S(1)} %exponential_multiply_fusion), kind=kOutput, calls=%fused_computation.38 | convolution fusion | flops 1077411840 | bytes 9437184 | tf_op jit(solution)/shard_map/dot_general | solution.py:38
  39.6 15.8 %collective-permute-done.1 = f32[520,512]{1,0:T(8,128)S(1)} collective-permute-done((f32[520,512]{1,0:T(8,128)S(1)}, f32[520,512]{1,0:T(8,128)S(1)}, u32[]{:S(2)}, u32[]{:S(2)}) %collective-permute-start.1) | collective-permute-done | bytes 1064992 | tf_op jit(solution)/shard_map/ppermute | solution.py:15
  55.3 0.7 fusion.98
  60.4 1.5 multiply_add_fusion.4
  61.9 1.1 maximum_maximum_fusion.1
  63.1 6.3 %collective-permute-start.2 = (f32[520,512]{1,0:T(8,128)}, f32[520,512]{1,0:T(8,128)}, u32[]{:S(2)}, u32[]{:S(2)}) collective-permute-start(f32[520,512]{1,0:T(8,128)} %maximum_maximum_fusion.1), channel_id=1, source_target_pairs={{0,2},{1,3},{2,4},{3,5},{4,6},{5,7},{6,8},{7,9},{8,10},{9,11},{10,... | collective-permute-start | bytes 3194888 | tf_op jit(solution)/shard_map/ppermute | solution.py:15
  69.3 21.9 %collective-permute-done.2 = f32[520,512]{1,0:T(8,128)} collective-permute-done((f32[520,512]{1,0:T(8,128)}, f32[520,512]{1,0:T(8,128)}, u32[]{:S(2)}, u32[]{:S(2)}) %collective-permute-start.2) | collective-permute-done | bytes 1064992 | tf_op jit(solution)/shard_map/ppermute | solution.py:15
  91.3 1.5 fusion.97
  94.8 1.5 multiply_add_fusion.3
  96.2 1.1 maximum_maximum_fusion.2
  97.4 5.4 %collective-permute-start.3 = (f32[520,512]{1,0:T(8,128)}, f32[520,512]{1,0:T(8,128)}, u32[]{:S(2)}, u32[]{:S(2)}) collective-permute-start(f32[520,512]{1,0:T(8,128)} %maximum_maximum_fusion.2), channel_id=1, source_target_pairs={{0,4},{1,5},{2,6},{3,7},{4,8},{5,9},{6,10},{7,11},{8,12},{9,13},{1... | collective-permute-start | bytes 3194888 | tf_op jit(solution)/shard_map/ppermute | solution.py:15
  102.7 22.3 %collective-permute-done.3 = f32[520,512]{1,0:T(8,128)} collective-permute-done((f32[520,512]{1,0:T(8,128)}, f32[520,512]{1,0:T(8,128)}, u32[]{:S(2)}, u32[]{:S(2)}) %collective-permute-start.3) | collective-permute-done | bytes 1064992 | tf_op jit(solution)/shard_map/ppermute | solution.py:15
  125.0 1.5 fusion.96
  128.6 1.5 multiply_add_fusion.2
  130.1 1.1 maximum_maximum_fusion.3
  131.3 28.0 %collective-permute-start.4 = (f32[520,512]{1,0:T(8,128)}, f32[520,512]{1,0:T(8,128)}, u32[]{:S(2)}, u32[]{:S(2)}) collective-permute-start(f32[520,512]{1,0:T(8,128)} %maximum_maximum_fusion.3), channel_id=1, source_target_pairs={{0,8},{1,9},{2,10},{3,11},{4,12},{5,13},{6,14},{7,15},{8,16},{9,17... | collective-permute-start | bytes 3194888 | tf_op jit(solution)/shard_map/ppermute | solution.py:15
  159.2 2.0 fusion.46
  161.2 2.0 fusion.32
  163.4 3.3 %fusion.45 = f32[1024,512]{1,0:T(8,128)} fusion(bf16[1024,512]{1,0:T(8,128)(2,1)S(1)} %convolution_convert_fusion, f32[520,512]{1,0:T(8,128)} %collective-permute-done.2), kind=kOutput, calls=%fused_computation.75 | convolution fusion | flops 537395200 | bytes 4194304 | tf_op jit(solution)/shard_map/dot_general | solution.py:45
  166.7 3.3 %fusion.34 = f32[1024,512]{1,0:T(8,128)} fusion(bf16[1024,512]{1,0:T(8,128)(2,1)S(1)} %convolution_convert_fusion, f32[520,512]{1,0:T(8,128)} %collective-permute-done.2), kind=kOutput, calls=%fused_computation.68 | convolution fusion | flops 537657344 | bytes 4194304 | tf_op jit(solution)/shard_map/dot_general | solution.py:46
  170.0 1.5 fusion.95
  173.4 1.5 multiply_add_fusion.1
  174.9 1.1 maximum_maximum_fusion.4
  176.0 7.7 %collective-permute-start.5 = (f32[520,512]{1,0:T(8,128)}, f32[520,512]{1,0:T(8,128)}, u32[]{:S(2)}, u32[]{:S(2)}) collective-permute-start(f32[520,512]{1,0:T(8,128)} %maximum_maximum_fusion.4), channel_id=1, source_target_pairs={{0,16},{1,17},{2,18},{3,19},{4,20},{5,21},{6,22},{7,23},{8,24},{9,... | collective-permute-start | bytes 3194888 | tf_op jit(solution)/shard_map/ppermute | solution.py:15
  183.7 1.9 fusion.44
  185.7 3.3 %fusion.36 = f32[1024,512]{1,0:T(8,128)} fusion(bf16[1024,512]{1,0:T(8,128)(2,1)S(1)} %convolution_convert_fusion, f32[520,512]{1,0:T(8,128)} %collective-permute-done.3), kind=kOutput, calls=%fused_computation.69 | convolution fusion | flops 537657344 | bytes 4194304 | tf_op jit(solution)/shard_map/dot_general | solution.py:46
  189.1 3.3 %fusion.43 = f32[1024,512]{1,0:T(8,128)} fusion(bf16[1024,512]{1,0:T(8,128)(2,1)S(1)} %convolution_convert_fusion, f32[520,512]{1,0:T(8,128)} %collective-permute-done.4), kind=kOutput, calls=%fused_computation.73 | convolution fusion | flops 537395200 | bytes 4194304 | tf_op jit(solution)/shard_map/dot_general | solution.py:45
  192.3 3.3 %fusion.38 = f32[1024,512]{1,0:T(8,128)} fusion(bf16[1024,512]{1,0:T(8,128)(2,1)S(1)} %convolution_convert_fusion, f32[520,512]{1,0:T(8,128)} %collective-permute-done.4), kind=kOutput, calls=%fused_computation.70 | convolution fusion | flops 537657344 | bytes 4194304 | tf_op jit(solution)/shard_map/dot_general | solution.py:46
  195.6 7.5 %collective-permute-done.5 = f32[520,512]{1,0:T(8,128)} collective-permute-done((f32[520,512]{1,0:T(8,128)}, f32[520,512]{1,0:T(8,128)}, u32[]{:S(2)}, u32[]{:S(2)}) %collective-permute-start.5) | collective-permute-done | bytes 1064992 | tf_op jit(solution)/shard_map/ppermute | solution.py:15
  203.2 1.3 slice.260
  205.3 2.1 fusion.40
  207.4 2.1 fusion.42
  209.5 0.5 copy-done.4
  210.0 4.8 %fusion.94 = (f32[1024]{0:T(1024)S(1)}, f32[1024,512]{1,0:T(8,128)S(1)}) fusion(f32[1024,512]{1,0:T(8,128)} %fusion.12, f32[1024]{0:T(1024)S(1)} %get-tuple-element.26, f32[1024,512]{1,0:T(8,128)S(1)} %copy-done.3, f32[1024,512]{1,0:T(8,128)S(1)} %copy-done.4, f32[]{:T(128)S(6)} %exp.97, f32[1024,512]{1,0:T(8,128)S(1)} %copy-done.5, ...), kind=kLoop, calls=%fused_computation.171 | loop fusion | flops 11009024 | bytes 25178144 | tf_op jit(solution)/shard_map/reduce_sum | solution.py:182
  214.9 0.4 multiply_reduce_fusion
  215.3 0.7 copy-done.9
  216.0 0.3 copy-done.13
  216.4 1.9 fusion.11
  (78 shorter events, 3.5 us)
Async XLA Ops:
  0.7 24.0 %collective-permute-start = (bf16[3,512]{1,0:T(4,128)(2,1)S(1)}, bf16[3,512]{1,0:T(4,128)(2,1)S(1)}, u32[]{:S(2)}, u32[]{:S(2)}) collective-permute-start(bf16[3,512]{1,0:T(4,128)(2,1)S(1)} %slice.190), channel_id=1, source_target_pairs={{0,1},{1,2},{2,3},{3,4},{4,5},{5,6},{6,7},{7,8},{8,9},{9,10},{10,1... | collective-permute-start | bytes 9224 | tf_op jit(solution)/shard_map/ppermute | solution.py:15
  19.0 5.7 %copy-start.10 = (bf16[1024,512]{1,0:T(8,128)(2,1)S(1)}, bf16[1024,512]{1,0:T(8,128)(2,1)}, u32[]{:S(2)}) copy-start(bf16[1024,512]{1,0:T(8,128)(2,1)} %param.9) | copy-start | bytes 3145732
  21.6 6.6 %copy-start.11 = (bf16[512,1024]{1,0:T(8,128)(2,1)}, bf16[512,1024]{1,0:T(8,128)(2,1)S(1)}, u32[]{:S(2)}) copy-start(bf16[512,1024]{1,0:T(8,128)(2,1)S(1)} %convolution_convert_fusion.1) | copy-start | bytes 3145732
  26.2 6.9 %copy-start.8 = (bf16[1024,512]{1,0:T(8,128)(2,1)}, bf16[1024,512]{1,0:T(8,128)(2,1)S(1)}, u32[]{:S(2)}) copy-start(bf16[1024,512]{1,0:T(8,128)(2,1)S(1)} %multiply_convert_fusion.1) | copy-start | bytes 3145732
  29.2 3.9 %copy-start.7 = (f32[512,512]{1,0:T(8,128)}, f32[512,512]{1,0:T(8,128)S(1)}, u32[]{:S(2)}) copy-start(f32[512,512]{1,0:T(8,128)S(1)} %convolution_add_fusion) | copy-start | bytes 3145732
  29.4 25.9 %collective-permute-start.1 = (f32[520,512]{1,0:T(8,128)S(1)}, f32[520,512]{1,0:T(8,128)S(1)}, u32[]{:S(2)}, u32[]{:S(2)}) collective-permute-start(f32[520,512]{1,0:T(8,128)S(1)} %maximum_maximum_fusion), channel_id=1, source_target_pairs={{0,1},{1,2},{2,3},{3,4},{4,5},{5,6},{6,7},{7,8},{8,9},{9,10},{10,1... | collective-permute-start | bytes 3194888 | tf_op jit(solution)/shard_map/ppermute | solution.py:15
  34.1 1.6 copy-start.12
  55.3 7.7 %copy-start = (f32[520,512]{1,0:T(8,128)}, f32[520,512]{1,0:T(8,128)S(1)}, u32[]{:S(2)}) copy-start(f32[520,512]{1,0:T(8,128)S(1)} %collective-permute-done.1) | copy-start | bytes 3194884
  63.1 28.2 %collective-permute-start.2 = (f32[520,512]{1,0:T(8,128)}, f32[520,512]{1,0:T(8,128)}, u32[]{:S(2)}, u32[]{:S(2)}) collective-permute-start(f32[520,512]{1,0:T(8,128)} %maximum_maximum_fusion.1), channel_id=1, source_target_pairs={{0,2},{1,3},{2,4},{3,5},{4,6},{5,7},{6,8},{7,9},{8,10},{9,11},{10,... | collective-permute-start | bytes 3194888 | tf_op jit(solution)/shard_map/ppermute | solution.py:15
  97.4 27.6 %collective-permute-start.3 = (f32[520,512]{1,0:T(8,128)}, f32[520,512]{1,0:T(8,128)}, u32[]{:S(2)}, u32[]{:S(2)}) collective-permute-start(f32[520,512]{1,0:T(8,128)} %maximum_maximum_fusion.2), channel_id=1, source_target_pairs={{0,4},{1,5},{2,6},{3,7},{4,8},{5,9},{6,10},{7,11},{8,12},{9,13},{1... | collective-permute-start | bytes 3194888 | tf_op jit(solution)/shard_map/ppermute | solution.py:15
  128.6 30.7 %copy-start.1 = (f32[520,512]{1,0:T(8,128)S(1)}, f32[520,512]{1,0:T(8,128)}, u32[]{:S(2)}) copy-start(f32[520,512]{1,0:T(8,128)} %copy-done) | copy-start | bytes 3194884
  131.3 30.0 %copy-start.2 = (f32[520,512]{1,0:T(8,128)S(1)}, f32[520,512]{1,0:T(8,128)}, u32[]{:S(2)}) copy-start(f32[520,512]{1,0:T(8,128)} %copy-done) | copy-start | bytes 3194884
  131.3 38.7 %collective-permute-start.4 = (f32[520,512]{1,0:T(8,128)}, f32[520,512]{1,0:T(8,128)}, u32[]{:S(2)}, u32[]{:S(2)}) collective-permute-start(f32[520,512]{1,0:T(8,128)} %maximum_maximum_fusion.3), channel_id=1, source_target_pairs={{0,8},{1,9},{2,10},{3,11},{4,12},{5,13},{6,14},{7,15},{8,16},{9,17... | collective-permute-start | bytes 3194888 | tf_op jit(solution)/shard_map/ppermute | solution.py:15
  176.0 27.1 %collective-permute-start.5 = (f32[520,512]{1,0:T(8,128)}, f32[520,512]{1,0:T(8,128)}, u32[]{:S(2)}, u32[]{:S(2)}) collective-permute-start(f32[520,512]{1,0:T(8,128)} %maximum_maximum_fusion.4), channel_id=1, source_target_pairs={{0,16},{1,17},{2,18},{3,19},{4,20},{5,21},{6,22},{7,23},{8,24},{9,... | collective-permute-start | bytes 3194888 | tf_op jit(solution)/shard_map/ppermute | solution.py:15
  205.2 4.2 %copy-start.5 = (f32[1024,512]{1,0:T(8,128)S(1)}, f32[1024,512]{1,0:T(8,128)}, u32[]{:S(2)}) copy-start(f32[1024,512]{1,0:T(8,128)} %fusion.45) | copy-start | bytes 6291460
  205.2 4.2 %copy-start.6 = (f32[1024,512]{1,0:T(8,128)S(1)}, f32[1024,512]{1,0:T(8,128)}, u32[]{:S(2)}) copy-start(f32[1024,512]{1,0:T(8,128)} %fusion.34) | copy-start | bytes 6291460
  207.4 2.1 copy-start.3
  207.4 2.6 %copy-start.4 = (f32[1024,512]{1,0:T(8,128)S(1)}, f32[1024,512]{1,0:T(8,128)}, u32[]{:S(2)}) copy-start(f32[1024,512]{1,0:T(8,128)} %fusion.32) | copy-start | bytes 6291460
  214.8 1.2 copy-start.9
  214.8 1.5 copy-start.13
  214.8 1.5 copy-start.14
  214.8 1.5 copy-start.15
